TPU v7x, 512 devices: a whole 4x4x16 slice. The times are simulated.
512 devices in a mesh: layer: 4 (over x), row: 8 (over y, core), col: 16 (over z).
Axes of the slice: x: 4, y: 4, z: 16, core: 2. Of those that a mesh axis runs over, the one named last changes fastest.
Arguments:
- density: bfloat16 [8192, 8192], P('row', 'col'), may hold values from -0.125 to 0.125
- hamiltonian: bfloat16 [8192, 8192], P('row', 'col'), may hold values from -6 to 6
- density_mask: int32 [128, 128], P('row', 'col'), may hold values from 0 to 1, as said below
- hamilton_mask: int32 [128, 128], P('row', 'col'), may hold values from 0 to 1, as said below
- filter_mask: int32 [128, 128], P('row', 'col'), may hold values from 0 to 1, as said below
Outputs:
- weighted: bfloat16 [8192, 8192], P('row', 'col')
Inputs may be any that keep to these rules, and one draw needn't show every extreme that they name: `density_mask`: each entry is 0 or 1; diagonal blocks are 1. `hamilton_mask`: each entry is 0 or 1; diagonal blocks are 1. `filter_mask`: each entry is 0 or 1; diagonal blocks are 1.
All inputs are finite; a program needn't handle non-finite values.
Results may differ from a plain program's by a relative error of at most 0.005.
Values may be sent and summed in bfloat16 or wider, within the bound.
No kernel may reach another device: no remote copies, remote signals or barrier semaphores. Data moves between devices by JAX's collectives and lax.ppermute only.
A program may use at most 64 MiB of HBM per device.

v0:
```python
import jax
import jax.numpy as jnp
from jax import lax
from jax.sharding import PartitionSpec as P

BS = 64


def expand_mask(mask_blocks):
    return jnp.repeat(jnp.repeat(mask_blocks, BS, axis=0), BS, axis=1).astype(jnp.bfloat16)


def inner_rows(matrix, groups, width, layer_pos):
    pieces = []
    stride = matrix.shape[0] // groups
    for group in range(groups):
        offset = group * stride + layer_pos * width
        pieces.append(lax.dynamic_slice_in_dim(matrix, offset, width, 0))
    return jnp.concatenate(pieces, axis=0)


def local(density, hamiltonian, density_mask, hamilton_mask, filter_mask):
    layers = lax.axis_size("layer")
    layer_pos = lax.axis_index("layer")
    groups = lax.axis_size("col") // lax.axis_size("row")
    tile_rows, tile_cols = density.shape
    width = tile_cols // layers
    masked_p = density * expand_mask(density_mask)
    masked_h = hamiltonian * expand_mask(hamilton_mask)
    h_inner = lax.all_gather(
        inner_rows(masked_h, groups, width, layer_pos), "row", axis=0, tiled=True
    )
    p_share = lax.dynamic_slice_in_dim(masked_p, layer_pos * width, width, 1)
    rows = h_inner
    partial_q = jnp.dot(
        lax.all_gather(p_share, "col", axis=1, tiled=True), rows, preferred_element_type=jnp.float32
    )
    summed_q = lax.psum_scatter(partial_q, "layer", scatter_dimension=1, tiled=True)
    filter_share = lax.dynamic_slice_in_dim(filter_mask, layer_pos * (width // BS), width // BS, 1)
    product = summed_q.astype(jnp.bfloat16) * expand_mask(filter_share)
    p_inner = lax.all_gather(
        inner_rows(masked_p, groups, width, layer_pos), "row", axis=0, tiled=True
    )
    rows = p_inner
    partial_w = jnp.dot(
        lax.all_gather(product, "col", axis=1, tiled=True), rows, preferred_element_type=jnp.float32
    )
    weighted = lax.psum(partial_w, "layer").astype(jnp.bfloat16)
    return weighted


def solution(mesh):
    placed = (P("row", "col"), P("row", "col"), P("row", "col"), P("row", "col"), P("row", "col"))
    return jax.shard_map(
        local, mesh=mesh, in_specs=placed, out_specs=P("row", "col"), check_vma=False
    )
```

profile of v0, /device:TPU:32, one launch (start us, length us, event | category | flops | bytes accessed | tf_op | source)
XLA Modules:
  0.0 339.1 jit_solution(550641898857958229)
XLA Ops:
  6.5 0.0 copy-start.1
  6.5 0.0 copy-start
  6.5 0.0 all-gather.7.cloned.1.call-start
  6.5 0.0 copy-start.2
  6.5 1.6 copy.9
  8.1 0.0 copy-done.1
  8.1 0.1 broadcast_in_dim.18
  8.2 0.1 convert_element_type.40
  8.3 0.0 copy-done
  8.4 0.5 copy.10
  8.9 0.0 copy-done.2
  8.9 0.1 broadcast_in_dim.20
  9.0 0.1 convert_element_type.43
  9.1 0.1 bitcast_multiply_fusion.1
  9.2 0.1 bitcast_multiply_fusion
  9.3 0.1 constant_dynamic-slice_fusion.1
  9.4 0.7 pad_maximum_fusion
  10.2 0.0 all-gather.7.cloned.1.call-update
  10.2 0.0 all-gather.5.cloned.1.call-start
  10.2 0.7 constant_dynamic-slice_fusion.5
  11.0 0.0 all-gather.5.cloned.1.call-update
  11.0 0.0 reduce-scatter.2.cloned.1.call-start
  11.0 37.9 %all-gather.7.cloned.1.call-done = bf16[2048,512]{0,1:T(8,128)(2,1)} async-done(((bf16[256,512]{0,1:T(8,128)(2,1)}), bf16[2048,512]{0,1:T(8,128)(2,1)}) %all-gather.7.cloned.1.call-update) | async-done | bytes 2097168 | tf_op jit(solution)/shard_map/all_gather | solution.py:30
  48.9 81.1 %all-gather.5.cloned.1.call-done = bf16[1024,2048]{0,1:T(8,128)(2,1)} async-done(((bf16[1024,128]{0,1:T(8,128)(2,1)}), bf16[1024,2048]{0,1:T(8,128)(2,1)}) %all-gather.5.cloned.1.call-update) | async-done | bytes 4194320 | tf_op jit(solution)/shard_map/all_gather | solution.py:36
  130.0 6.5 %fusion.2 = f32[1024,512]{0,1:T(8,128)} fusion(bf16[2048,512]{0,1:T(8,128)(2,1)} %all-gather.7.cloned.1.call-done, bf16[1024,2048]{0,1:T(8,128)(2,1)} %all-gather.5.cloned.1.call-done), kind=kOutput, calls=%fused_computation.13 | convolution fusion | flops 2147483648 | bytes 8388608 | tf_op jit(solution)/shard_map/dot_general | solution.py:35
  136.5 0.0 reduce-scatter.2.cloned.1.call-update
  136.5 0.0 all-gather.11.cloned.1.call-start
  136.6 0.8 pad_maximum_fusion.1
  137.3 0.0 all-gather.11.cloned.1.call-update
  137.4 0.0 all-gather.9.cloned.1.call-start
  137.4 0.7 fusion
  138.1 0.1 broadcast_in_dim.22
  138.2 0.1 convert_element_type.47
  138.3 32.2 %reduce-scatter.2.cloned.1.call-done = f32[1024,128]{0,1:T(8,128)} async-done(((f32[1024,512]{0,1:T(8,128)}), f32[1024,128]{0,1:T(8,128)}) %reduce-scatter.2.cloned.1.call-update) | async-done | bytes 524304 | tf_op jit(solution)/shard_map/reduce_scatter | solution.py:38
  170.5 1.8 bitcast_multiply_fusion.2
  172.3 0.0 all-gather.9.cloned.1.call-update
  172.3 34.5 %all-gather.11.cloned.1.call-done = bf16[2048,512]{0,1:T(8,128)(2,1)} async-done(((bf16[256,512]{0,1:T(8,128)(2,1)}), bf16[2048,512]{0,1:T(8,128)(2,1)}) %all-gather.11.cloned.1.call-update) | async-done | bytes 2097168 | tf_op jit(solution)/shard_map/all_gather | solution.py:41
  206.8 80.9 %all-gather.9.cloned.1.call-done = bf16[1024,2048]{0,1:T(8,128)(2,1)} async-done(((bf16[1024,128]{0,1:T(8,128)(2,1)}), bf16[1024,2048]{0,1:T(8,128)(2,1)}) %all-gather.9.cloned.1.call-update) | async-done | bytes 4194320 | tf_op jit(solution)/shard_map/all_gather | solution.py:46
  287.7 5.2 %fusion.1 = f32[1024,512]{1,0:T(8,128)S(1)} fusion(bf16[1024,2048]{0,1:T(8,128)(2,1)} %all-gather.9.cloned.1.call-done, bf16[2048,512]{0,1:T(8,128)(2,1)} %all-gather.11.cloned.1.call-done), kind=kOutput, calls=%fused_computation.12 | convolution fusion | flops 2147483648 | bytes 8388608 | tf_op jit(solution)/shard_map/dot_general | solution.py:45
  292.9 39.7 %all-reduce.1 = bf16[1024,512]{1,0:T(8,128)(2,1)} all-reduce(f32[1024,512]{1,0:T(8,128)S(1)} %fusion.1), channel_id=1, replica_groups=mesh['layer'=4,'row'=8,'col'=16] {'layer'}, use_global_device_ids=true, to_apply=%region_1.0 | all-reduce | flops 524288 | bytes 3145728 | tf_op jit(solution)/shard_map/psum | solution.py:48
  (2 shorter events, 0.0 us)
Async XLA Ops:
  6.5 1.6 copy-start.1
  6.5 1.8 copy-start
  6.5 42.4 %all-gather.7.cloned.1.call-start = ((), (), s32[]{:S(2)}) async-start(), calls=%async_computation.2 | async-start | bytes 2359296 | tf_op jit(solution)/shard_map/all_gather | solution.py:30
  6.5 2.4 copy-start.2
  10.2 119.8 %all-gather.5.cloned.1.call-start = ((), (), s32[]{:S(2)}) async-start(), calls=%async_computation.1 | async-start | bytes 4456448 | tf_op jit(solution)/shard_map/all_gather | solution.py:36
  11.0 159.5 %reduce-scatter.2.cloned.1.call-start = ((), (), s32[]{:S(2)}) async-start(), calls=%async_computation.3 | async-start | bytes 2621440 | tf_op jit(solution)/shard_map/reduce_scatter | solution.py:38
  136.5 70.2 %all-gather.11.cloned.1.call-start = ((), (), s32[]{:S(2)}) async-start(), calls=%async_computation.5 | async-start | bytes 2359296 | tf_op jit(solution)/shard_map/all_gather | solution.py:41
  137.4 150.3 %all-gather.9.cloned.1.call-start = ((), (), s32[]{:S(2)}) async-start(), calls=%async_computation.4 | async-start | bytes 4456448 | tf_op jit(solution)/shard_map/all_gather | solution.py:46
Sparse Core Ops, SparseCore 0:
  10.3 38.5 all-gather.6
  51.0 78.9 all-gather.4
  136.6 33.7 reduce-scatter.1
  172.4 34.2 all-gather.10
  208.7 78.9 all-gather.8
where the time goes:
time: 339 us
  waiting for transfers between devices  267 us (79%)
  blocking collectives  39.7 us (12%)
  between operations  13.3 us (4%)
  matrix products  11.7 us (3%)
  other arithmetic  4.13 us (1%)
  local copies, waits for them, and re-layouts  3.51 us (1%)
    all_gather x1, waiting for transfers between devices, local(): lax.all_gather(p_share, 'col', axis=1, tiled=True)  81.1 us
    all_gather x1, waiting for transfers between devices, local(): lax.all_gather(product, 'col', axis=1, tiled=True)  80.9 us
    psum x1, blocking collectives, local(): weighted = lax.psum(partial_w, 'layer').astype(jnp.bfloat16)  39.7 us
    all_gather x1, waiting for transfers between devices, local(): lax.all_gather(inner_rows(masked_h, groups, width, layer_pos), 'row', axi...  37.9 us
    all_gather x1, waiting for transfers between devices, local(): lax.all_gather(inner_rows(masked_p, groups, width, layer_pos), 'row', axi...  34.5 us
    reduce_scatter x1, waiting for transfers between devices, local(): lax.psum_scatter(partial_q, 'layer', scatter_dimension=1, tiled=True)  32.2 us
  transfers between devices with their start and end apart: 5, of which 5 were waited for; matrix products, arithmetic and copies ran while one was open for 1% of the time, Pallas kernels for 0%

commit v1 on v0

--- a/solution.py
+++ b/solution.py
@@ -1,9 +1,19 @@
+import functools
 import jax
 import jax.numpy as jnp
 from jax import lax
 from jax.sharding import PartitionSpec as P
+from jax.lax import all_gather
 
 BS = 64
+
+
+def build_files_for(frame, chip_axis):
+    inter = jnp.sum(all_gather(frame, chip_axis), 0)
+    return inter
+
+
+create_weights = functools.partial(build_files_for, chip_axis="layer")
 
 
 def expand_mask(mask_blocks):
@@ -45,7 +55,7 @@
     partial_w = jnp.dot(
         lax.all_gather(product, "col", axis=1, tiled=True), rows, preferred_element_type=jnp.float32
     )
-    weighted = lax.psum(partial_w, "layer").astype(jnp.bfloat16)
+    weighted = create_weights(partial_w).astype(jnp.bfloat16)
     return weighted
 
 

time: 339 us -> 395 us (1.17)
  the two profiles are of different devices: /device:TPU:32 before, /device:TPU:1 now
where the time goes in v1:
time: 395 us
  waiting for transfers between devices  355 us (90%)
  between operations  13.6 us (3%)
  matrix products  13.1 us (3%)
  other arithmetic  9.81 us (2%)
    all_gather x1, waiting for transfers between devices, build_files_for(): inter = jnp.sum(all_gather(frame, chip_axis), 0)  95.9 us
    all_gather x1, waiting for transfers between devices, local(): lax.all_gather(p_share, 'col', axis=1, tiled=True)  71.5 us
    all_gather x1, waiting for transfers between devices, local(): lax.all_gather(product, 'col', axis=1, tiled=True)  71.3 us
    reduce_scatter x1, waiting for transfers between devices, local(): lax.psum_scatter(partial_q, 'layer', scatter_dimension=1, tiled=True)  40.9 us
    all_gather x1, waiting for transfers between devices, local(): lax.all_gather(inner_rows(masked_h, groups, width, layer_pos), 'row', axi...  39.9 us
    all_gather x1, waiting for transfers between devices, local(): lax.all_gather(inner_rows(masked_p, groups, width, layer_pos), 'row', axi...  35.4 us
  transfers between devices with their start and end apart: 6, of which 6 were waited for; matrix products, arithmetic and copies ran while one was open for 1% of the time, Pallas kernels for 0%

profile of v1, /device:TPU:1, one launch (start us, length us, event | category | flops | bytes accessed | tf_op | source)
XLA Modules:
  0.0 395.2 jit_solution(17550901405232977846)
XLA Ops:
  6.5 0.0 copy-start.1
  6.5 0.0 copy-start
  6.5 0.0 all-gather.9.cloned.1.call-start
  6.5 0.0 copy-start.2
  6.5 1.6 copy.9
  8.1 0.0 copy-done.1
  8.1 0.1 broadcast_in_dim.18
  8.2 0.1 convert_element_type.40
  8.3 0.0 copy-done
  8.4 0.5 copy.10
  8.9 0.0 copy-done.2
  8.9 0.1 broadcast_in_dim.20
  9.0 0.1 convert_element_type.43
  9.1 0.1 bitcast_multiply_fusion.1
  9.2 0.1 bitcast_multiply_fusion
  9.3 0.1 constant_dynamic-slice_fusion.1
  9.4 0.7 pad_maximum_fusion
  10.2 0.0 all-gather.9.cloned.1.call-update
  10.2 0.0 all-gather.7.cloned.1.call-start
  10.2 0.7 constant_dynamic-slice_fusion.5
  11.0 0.0 all-gather.7.cloned.1.call-update
  11.0 0.0 reduce-scatter.2.cloned.1.call-start
  11.0 39.9 %all-gather.9.cloned.1.call-done = bf16[2048,512]{0,1:T(8,128)(2,1)} async-done(((bf16[256,512]{0,1:T(8,128)(2,1)}), bf16[2048,512]{0,1:T(8,128)(2,1)}) %all-gather.9.cloned.1.call-update) | async-done | bytes 2097168 | tf_op jit(solution)/shard_map/all_gather | solution.py:40
  51.0 71.5 %all-gather.7.cloned.1.call-done = bf16[1024,2048]{0,1:T(8,128)(2,1)} async-done(((bf16[1024,128]{0,1:T(8,128)(2,1)}), bf16[1024,2048]{0,1:T(8,128)(2,1)}) %all-gather.7.cloned.1.call-update) | async-done | bytes 4194320 | tf_op jit(solution)/shard_map/all_gather | solution.py:46
  122.5 6.5 %fusion.2 = f32[1024,512]{0,1:T(8,128)} fusion(bf16[2048,512]{0,1:T(8,128)(2,1)} %all-gather.9.cloned.1.call-done, bf16[1024,2048]{0,1:T(8,128)(2,1)} %all-gather.7.cloned.1.call-done), kind=kOutput, calls=%fused_computation.13 | convolution fusion | flops 2147483648 | bytes 8388608 | tf_op jit(solution)/shard_map/dot_general | solution.py:45
  129.0 0.0 reduce-scatter.2.cloned.1.call-update
  129.0 0.0 all-gather.13.cloned.1.call-start
  129.0 0.7 pad_maximum_fusion.1
  129.8 0.0 all-gather.13.cloned.1.call-update
  129.8 0.0 all-gather.11.cloned.1.call-start
  129.9 0.7 fusion
  130.6 0.1 broadcast_in_dim.22
  130.6 0.1 convert_element_type.47
  130.7 40.9 %reduce-scatter.2.cloned.1.call-done = f32[1024,128]{0,1:T(8,128)} async-done(((f32[1024,512]{0,1:T(8,128)}), f32[1024,128]{0,1:T(8,128)}) %reduce-scatter.2.cloned.1.call-update) | async-done | bytes 524304 | tf_op jit(solution)/shard_map/reduce_scatter | solution.py:48
  171.6 1.8 bitcast_multiply_fusion.2
  173.4 0.0 all-gather.11.cloned.1.call-update
  173.4 0.0 all-gather.15.cloned.1.call-start
  173.4 35.4 %all-gather.13.cloned.1.call-done = bf16[2048,512]{0,1:T(8,128)(2,1)} async-done(((bf16[256,512]{0,1:T(8,128)(2,1)}), bf16[2048,512]{0,1:T(8,128)(2,1)}) %all-gather.13.cloned.1.call-update) | async-done | bytes 2097168 | tf_op jit(solution)/shard_map/all_gather | solution.py:51
  208.8 71.3 %all-gather.11.cloned.1.call-done = bf16[1024,2048]{0,1:T(8,128)(2,1)} async-done(((bf16[1024,128]{0,1:T(8,128)(2,1)}), bf16[1024,2048]{0,1:T(8,128)(2,1)}) %all-gather.11.cloned.1.call-update) | async-done | bytes 4194320 | tf_op jit(solution)/shard_map/all_gather | solution.py:56
  280.2 6.6 %fusion.1 = f32[1024,512]{1,0:T(8,128)} fusion(bf16[1024,2048]{0,1:T(8,128)(2,1)} %all-gather.11.cloned.1.call-done, bf16[2048,512]{0,1:T(8,128)(2,1)} %all-gather.13.cloned.1.call-done), kind=kOutput, calls=%fused_computation.12 | convolution fusion | flops 2147483648 | bytes 8388608 | tf_op jit(solution)/shard_map/dot_general | solution.py:55
  286.8 0.0 all-gather.15.cloned.1.call-update
  286.8 95.9 %all-gather.15.cloned.1.call-done = f32[4096,512]{1,0:T(8,128)} async-done(((f32[1024,512]{1,0:T(8,128)}), f32[4096,512]{1,0:T(8,128)}) %all-gather.15.cloned.1.call-update) | async-done | bytes 8388624 | tf_op jit(solution)/shard_map/all_gather | solution.py:12
  382.7 5.7 %reduce_sum.9 = bf16[1024,512]{1,0:T(8,128)(2,1)} reduce(f32[4,1024,512]{2,1,0:T(8,128)} %bitcast.17, f32[]{:T(128)} %constant.21.clone.1), dimensions={0}, to_apply=%region_1.0 | reduce | flops 1572864 | bytes 9437188 | tf_op jit(solution)/shard_map/reduce_sum | solution.py:12
  (2 shorter events, 0.0 us)
Async XLA Ops:
  6.5 1.6 copy-start.1
  6.5 1.8 copy-start
  6.5 44.4 %all-gather.9.cloned.1.call-start = ((), (), s32[]{:S(2)}) async-start(), calls=%async_computation.2 | async-start | bytes 2359296 | tf_op jit(solution)/shard_map/all_gather | solution.py:40
  6.5 2.4 copy-start.2
  10.2 112.3 %all-gather.7.cloned.1.call-start = ((), (), s32[]{:S(2)}) async-start(), calls=%async_computation.1 | async-start | bytes 4456448 | tf_op jit(solution)/shard_map/all_gather | solution.py:46
  11.0 160.6 %reduce-scatter.2.cloned.1.call-start = ((), (), s32[]{:S(2)}) async-start(), calls=%async_computation.3 | async-start | bytes 2621440 | tf_op jit(solution)/shard_map/reduce_scatter | solution.py:48
  129.0 79.8 %all-gather.13.cloned.1.call-start = ((), (), s32[]{:S(2)}) async-start(), calls=%async_computation.5 | async-start | bytes 2359296 | tf_op jit(solution)/shard_map/all_gather | solution.py:51
  129.8 150.4 %all-gather.11.cloned.1.call-start = ((), (), s32[]{:S(2)}) async-start(), calls=%async_computation.4 | async-start | bytes 4456448 | tf_op jit(solution)/shard_map/all_gather | solution.py:56
  173.4 209.3 %all-gather.15.cloned.1.call-start = ((), (), s32[]{:S(2)}) async-start(), calls=%async_computation.6 | async-start | bytes 10485760 | tf_op jit(solution)/shard_map/all_gather | solution.py:12
Sparse Core Ops, SparseCore 0:
  10.3 40.6 all-gather.8
  53.1 69.3 all-gather.6
  129.1 42.4 reduce-scatter.1
  173.6 35.2 all-gather.12
  210.8 69.3 all-gather.10
  286.9 95.7 all-gather.14

commit v2 on v0

--- a/solution.py
+++ b/solution.py
@@ -38,9 +38,11 @@
     summed_q = lax.psum_scatter(partial_q, "layer", scatter_dimension=1, tiled=True)
     filter_share = lax.dynamic_slice_in_dim(filter_mask, layer_pos * (width // BS), width // BS, 1)
     product = summed_q.astype(jnp.bfloat16) * expand_mask(filter_share)
-    p_inner = lax.all_gather(
-        inner_rows(masked_p, groups, width, layer_pos), "row", axis=0, tiled=True
-    )
+    block_here = inner_rows(masked_p, groups, width, layer_pos)
+    all_values = lax.axis_size("row")
+    part_next = jnp.stack([block_here] * all_values)
+    answer = lax.all_to_all(part_next, axis_name="row", split_axis=0, concat_axis=0)
+    p_inner = jnp.concatenate(answer, axis=0)
     rows = p_inner
     partial_w = jnp.dot(
         lax.all_gather(product, "col", axis=1, tiled=True), rows, preferred_element_type=jnp.float32

time: 339 us -> 303 us (0.89)
  waiting for transfers between devices: 267 us -> 198 us
  blocking collectives: 39.7 us -> 71.7 us
    all_gather x1, waiting for transfers between devices: 80.9 us -> 46.3 us  [local(): lax.all_gather(product, 'col', axis=1, tiled=True)]
    all_gather x1 -> x0, waiting for transfers between devices: 34.5 us -> none  [local(): lax.all_gather(inner_rows(masked_p, groups, width, layer_pos), 'row', axi...]
    all_to_all x0 -> x1, blocking collectives: none -> 31.3 us  [local(): lax.all_to_all(part_next, axis_name='row', split_axis=0, concat_axis=0)]
  transfers between devices with their start and end apart: 5 -> 4, of which waited for: 5 -> 4; matrix products, arithmetic and copies ran while one was open for 1% -> 1% of each run, Pallas kernels for 0% -> 0%
where the time goes in v2:
time: 303 us
  waiting for transfers between devices  198 us (65%)
  blocking collectives  71.7 us (24%)
  between operations  13.3 us (4%)
  matrix products  12.4 us (4%)
  local copies, waits for them, and re-layouts  3.84 us (1%)
  other arithmetic  3.4 us (1%)
    all_gather x1, waiting for transfers between devices, local(): lax.all_gather(p_share, 'col', axis=1, tiled=True)  81.1 us
    all_gather x1, waiting for transfers between devices, local(): lax.all_gather(product, 'col', axis=1, tiled=True)  46.3 us
    psum x1, blocking collectives, local(): weighted = lax.psum(partial_w, 'layer').astype(jnp.bfloat16)  40.4 us
    all_gather x1, waiting for transfers between devices, local(): lax.all_gather(inner_rows(masked_h, groups, width, layer_pos), 'row', axi...  37.9 us
    reduce_scatter x1, waiting for transfers between devices, local(): lax.psum_scatter(partial_q, 'layer', scatter_dimension=1, tiled=True)  33.1 us
    all_to_all x1, blocking collectives, local(): lax.all_to_all(part_next, axis_name='row', split_axis=0, concat_axis=0)  31.3 us
    dot_general x1, matrix products, local(): jnp.dot(lax.all_gather(p_share, 'col', axis=1, tiled=True), rows, preferr...  6.5 us
  transfers between devices with their start and end apart: 4, of which 4 were waited for; matrix products, arithmetic and copies ran while one was open for 1% of the time, Pallas kernels for 0%

profile of v2, /device:TPU:32, one launch (start us, length us, event | category | flops | bytes accessed | tf_op | source)
XLA Modules:
  0.0 303.1 jit_solution(6221576494593236263)
XLA Ops:
  6.5 0.0 copy-start.1
  6.5 0.0 copy-start
  6.5 0.0 all-gather.6.cloned.1.call-start
  6.5 0.0 copy-start.2
  6.5 1.6 copy.9
  8.1 0.0 copy-done.1
  8.1 0.1 broadcast_in_dim.18
  8.2 0.1 convert_element_type.40
  8.3 0.0 copy-done
  8.4 0.5 copy.10
  8.9 0.0 copy-done.2
  8.9 0.1 broadcast_in_dim.20
  9.0 0.1 convert_element_type.43
  9.1 0.1 bitcast_multiply_fusion.1
  9.2 0.1 bitcast_multiply_fusion
  9.3 0.1 constant_dynamic-slice_fusion.1
  9.4 0.7 pad_maximum_fusion
  10.2 0.0 all-gather.6.cloned.1.call-update
  10.2 0.0 all-gather.4.cloned.1.call-start
  10.2 0.7 constant_dynamic-slice_fusion.5
  11.0 0.0 all-gather.4.cloned.1.call-update
  11.0 0.0 reduce-scatter.2.cloned.1.call-start
  11.0 37.9 %all-gather.6.cloned.1.call-done = bf16[2048,512]{0,1:T(8,128)(2,1)} async-done(((bf16[256,512]{0,1:T(8,128)(2,1)}), bf16[2048,512]{0,1:T(8,128)(2,1)}) %all-gather.6.cloned.1.call-update) | async-done | bytes 2097168 | tf_op jit(solution)/shard_map/all_gather | solution.py:30
  48.9 81.1 %all-gather.4.cloned.1.call-done = bf16[1024,2048]{0,1:T(8,128)(2,1)} async-done(((bf16[1024,128]{0,1:T(8,128)(2,1)}), bf16[1024,2048]{0,1:T(8,128)(2,1)}) %all-gather.4.cloned.1.call-update) | async-done | bytes 4194320 | tf_op jit(solution)/shard_map/all_gather | solution.py:36
  130.0 6.5 %fusion.2 = f32[1024,512]{0,1:T(8,128)} fusion(bf16[2048,512]{0,1:T(8,128)(2,1)} %all-gather.6.cloned.1.call-done, bf16[1024,2048]{0,1:T(8,128)(2,1)} %all-gather.4.cloned.1.call-done), kind=kOutput, calls=%fused_computation.13 | convolution fusion | flops 2147483648 | bytes 8388608 | tf_op jit(solution)/shard_map/dot_general | solution.py:35
  136.5 0.0 reduce-scatter.2.cloned.1.call-update
  136.5 0.0 all-gather.8.cloned.1.call-start
  136.6 0.7 fusion
  137.3 0.1 broadcast_in_dim.22
  137.4 0.1 convert_element_type.47
  137.4 33.1 %reduce-scatter.2.cloned.1.call-done = f32[1024,128]{0,1:T(8,128)} async-done(((f32[1024,512]{0,1:T(8,128)}), f32[1024,128]{0,1:T(8,128)}) %reduce-scatter.2.cloned.1.call-update) | async-done | bytes 524304 | tf_op jit(solution)/shard_map/reduce_scatter | solution.py:38
  170.5 1.8 bitcast_multiply_fusion.2
  172.3 0.0 all-gather.8.cloned.1.call-update
  172.4 0.1 copy.11
  172.5 0.2 stack.2
  172.7 31.3 %all_to_all.5 = bf16[8,256,512]{2,1,0:T(8,128)(2,1)S(1)} all-to-all(bf16[8,256,512]{2,1,0:T(8,128)(2,1)S(1)} %stack.2), channel_id=1, replica_groups=mesh['layer'=4,'row'=8,'col'=16] {'row'}, dimensions={0} | all-to-all | bytes 4194304 | tf_op jit(solution)/shard_map/all_to_all | solution.py:44
  204.0 46.3 %all-gather.8.cloned.1.call-done = bf16[1024,2048]{0,1:T(8,128)(2,1)} async-done(((bf16[1024,128]{0,1:T(8,128)(2,1)}), bf16[1024,2048]{0,1:T(8,128)(2,1)}) %all-gather.8.cloned.1.call-update) | async-done | bytes 4194320 | tf_op jit(solution)/shard_map/all_gather | solution.py:48
  250.3 5.9 %fusion.1 = f32[1024,512]{1,0:T(8,128)} fusion(bf16[1024,2048]{0,1:T(8,128)(2,1)} %all-gather.8.cloned.1.call-done, bf16[2048,512]{1,0:T(8,128)(2,1)S(1)} %bitcast.17), kind=kOutput, calls=%fused_computation.12 | convolution fusion | flops 2147483648 | bytes 8388608 | tf_op jit(solution)/shard_map/dot_general | solution.py:47
  256.2 40.4 %all-reduce.1 = bf16[1024,512]{1,0:T(8,128)(2,1)} all-reduce(f32[1024,512]{1,0:T(8,128)} %fusion.1), channel_id=1, replica_groups=mesh['layer'=4,'row'=8,'col'=16] {'layer'}, use_global_device_ids=true, to_apply=%region_1.0 | all-reduce | flops 524288 | bytes 3145728 | tf_op jit(solution)/shard_map/psum | solution.py:50
  (3 shorter events, 0.0 us)
Async XLA Ops:
  6.5 1.6 copy-start.1
  6.5 1.8 copy-start
  6.5 42.4 %all-gather.6.cloned.1.call-start = ((), (), s32[]{:S(2)}) async-start(), calls=%async_computation.3 | async-start | bytes 2359296 | tf_op jit(solution)/shard_map/all_gather | solution.py:30
  6.5 2.4 copy-start.2
  10.2 119.8 %all-gather.4.cloned.1.call-start = ((), (), s32[]{:S(2)}) async-start(), calls=%async_computation.2 | async-start | bytes 4456448 | tf_op jit(solution)/shard_map/all_gather | solution.py:36
  11.0 159.6 %reduce-scatter.2.cloned.1.call-start = ((), (), s32[]{:S(2)}) async-start(), calls=%async_computation.4 | async-start | bytes 2621440 | tf_op jit(solution)/shard_map/reduce_scatter | solution.py:38
  136.5 113.8 %all-gather.8.cloned.1.call-start = ((), (), s32[]{:S(2)}) async-start(), calls=%async_computation.5 | async-start | bytes 4456448 | tf_op jit(solution)/shard_map/all_gather | solution.py:48
Sparse Core Ops, SparseCore 0:
  10.3 38.5 all-gather.5
  51.0 78.9 all-gather.3
  136.7 33.8 reduce-scatter.1
  172.5 77.7 all-gather.7
